TPU v7x, 256 devices: a whole 4x4x8 slice. The times are simulated.
256 devices in a mesh: dp: 16 (over y, z_hi, core), tensor: 16 (over z_lo, x).
Axes of the slice: x: 4, y: 4, z: 8 (z_hi: 2, z_lo: 4; z = z_hi * 4 + z_lo), core: 2. Of those that a mesh axis runs over, the one named last changes fastest.
Arguments:
- token_ids: int32 [4096], P('dp'), may hold values from 0 to 128255
- attn_heads: bfloat16 [4096, 8192], P('dp', 'tensor'), may hold values from -6 to 6
- out_proj: bfloat16 [8192, 8192], P('tensor'), may hold values from -0.0625 to 0.0625
- residual: bfloat16 [4096, 8192], P(('dp', 'tensor')), may hold values from -6 to 6
- norm_gain: float32 [8192], replicated, may hold values from 0.5 to 1.5
- twist_in: bfloat16 [8192, 8192], P('dp', 'tensor'), may hold values from -0.0625 to 0.0625
- twist_out: float32 [8192], P('tensor'), may hold values from -0.26516503 to 0.26516503
- token_bias: float32 [128256], replicated, may hold values from -4 to 262
- toxicity: int32 [16], P('dp'), may hold values from 1 to 4
- prompt_len: int32 [16], P('dp'), may hold values from 1 to 128
Outputs:
- twist_vals: float32 [4096], P('dp')
- grad_in: float32 [8192, 8192], P('dp', 'tensor')
- grad_out: float32 [8192], P('tensor')
- grad_bias: float32 [128256], P('dp')
All inputs are finite; a program needn't handle non-finite values.
Results may differ from a plain program's by a relative error of at most 0.033.
Values may be sent and summed in bfloat16 or wider, within the bound.
No kernel may reach another device: no remote copies, remote signals or barrier semaphores. Data moves between devices by JAX's collectives and lax.ppermute only.
A program may use at most 128 MiB of HBM per device.

v0:
```python
import jax
import jax.numpy as jnp
from jax import lax
from jax.sharding import PartitionSpec as P


def merged_2(value, axis, join):
    pieces = jax.tree.map(lambda part: lax.all_gather(part, axis), value)
    head = jax.tree.map(lambda part: part[0], pieces)
    tail = jax.tree.map(lambda part: part[1:], pieces)
    total, _ = lax.scan(lambda total, share: (join(total, share), None), head, tail)
    return total


def normalize(hidden, norm_gain):
    values = hidden.astype(jnp.float32)
    scaled = lax.rsqrt(jnp.mean(values * values, axis=-1, keepdims=True) + 1e-05)
    return (values * scaled * norm_gain[None, :]).astype(jnp.bfloat16)


def combine(earlier, later):
    high_one, sum_one, lab_one = earlier
    high_two, sum_two, lab_two = later
    highest = jnp.maximum(high_one, high_two)
    merged = sum_one * jnp.exp(high_one - highest) + sum_two * jnp.exp(high_two - highest)
    return (highest, merged, lab_one + lab_two)


def local(
    token_ids,
    attn_heads,
    out_proj,
    residual,
    norm_gain,
    twist_in,
    twist_out,
    token_bias,
    toxicity,
    prompt_len,
):
    seq_len = attn_heads.shape[0]
    vocab_size = token_bias.shape[0]
    partial_sum = jnp.dot(attn_heads, out_proj, preferred_element_type=jnp.float32)
    summed = lax.psum(partial_sum.astype(jnp.bfloat16), "tensor").astype(jnp.float32)
    resid_all = lax.all_gather(residual, "tensor", axis=0, tiled=True)
    hidden = (resid_all.astype(jnp.float32) + summed).astype(jnp.bfloat16)
    normed = normalize(hidden, norm_gain)
    columns = normed
    pre_act = jnp.dot(
        columns,
        lax.all_gather(twist_in, "dp", axis=0, tiled=True),
        preferred_element_type=jnp.float32,
    )
    active = jax.nn.silu(pre_act)
    partial_psi = jnp.dot(active, twist_out, precision=lax.Precision.HIGHEST)
    twist_vals = lax.psum(partial_psi, "tensor") + token_bias[token_ids]
    live = jnp.arange(seq_len) >= prompt_len[0]
    live_float = live.astype(jnp.float32)
    levels = toxicity[0].astype(jnp.float32) * live_float
    local_high = jnp.where(live, twist_vals, -1e30)
    highest, totals, lab_sum = merged_2((local_high, live_float, levels), "dp", combine)
    expo = jnp.where(live, jnp.exp(jnp.where(live, twist_vals - highest, -80.0)), 0.0)
    weights = (expo / jnp.maximum(totals, 1.0) - levels / jnp.maximum(lab_sum, 1.0)) / seq_len
    grad_out = lax.psum(jnp.dot(weights, active, precision=lax.Precision.HIGHEST), "dp")
    local_bias = jnp.zeros((vocab_size,), jnp.float32).at[token_ids].add(weights)
    grad_bias = lax.psum_scatter(
        local_bias.astype(jnp.bfloat16), "dp", scatter_dimension=0, tiled=True
    ).astype(jnp.float32)
    sigma = jax.nn.sigmoid(pre_act)
    d_pre = (
        weights[:, None] * twist_out[None, :] * sigma * (1.0 + pre_act * (1.0 - sigma))
    ).astype(jnp.bfloat16)
    contract = (((0,), (0,)), ((), ()))
    columns = normed
    grad_in = lax.psum_scatter(
        lax.dot_general(columns, d_pre, contract, preferred_element_type=jnp.float32).astype(
            jnp.bfloat16
        ),
        "dp",
        scatter_dimension=0,
        tiled=True,
    ).astype(jnp.float32)
    return (twist_vals, grad_in, grad_out, grad_bias)


def solution(mesh):
    placed = (
        P("dp"),
        P("dp", "tensor"),
        P("tensor", None),
        P(("dp", "tensor"), None),
        P(),
        P("dp", "tensor"),
        P("tensor"),
        P(),
        P("dp"),
        P("dp"),
    )
    return jax.shard_map(
        local,
        mesh=mesh,
        in_specs=placed,
        out_specs=(P("dp"), P("dp", "tensor"), P("tensor"), P("dp")),
        check_vma=False,
    )
```

profile of v0, /device:TPU:2, one launch (start us, length us, event | category | flops | bytes accessed | tf_op | source)
XLA Modules:
  0.0 797.6 jit_solution(13153336247750633944)
XLA Ops:
  7.2 0.0 copy-start
  7.2 0.0 copy-start.2
  7.2 0.0 all-reduce.4.cloned.1.call-start
  7.2 7.8 convolution_convert_fusion.1
  15.1 0.0 copy-start.3
  15.1 0.0 all-reduce.4.cloned.1.call-update
  15.1 0.0 all-gather.7.cloned.1.call-start
  15.1 0.7 all-gather.7.cloned.1.call-update
  15.8 0.0 all-gather.9.cloned.1.call-start
  15.9 0.7 all-gather.9.cloned.1.call-update
  16.6 0.0 all-reduce.6.cloned.1.call-start
  17.9 33.4 %all-gather.3 = f32[16,1,256]{2,1,0:T(1,128)S(1)} all-gather(f32[1,1,256]{2,1,0:T(1,128)S(1)} %fusion.13), channel_id=1, replica_groups=mesh['dp'=16,'tensor'=16] {'dp'}, dimensions={0}, use_global_device_ids=true | all-gather | bytes 17408 | tf_op jit(solution)/shard_map/all_gather | solution.py:8
  51.4 24.1 %all-gather.2 = f32[16,1,256]{2,1,0:T(1,128)S(1)} all-gather(f32[1,1,256]{2,1,0:T(1,128)S(1)} %fusion.14), channel_id=1, replica_groups=mesh['dp'=16,'tensor'=16] {'dp'}, dimensions={0}, use_global_device_ids=true | all-gather | bytes 17408 | tf_op jit(solution)/shard_map/all_gather | solution.py:8
  75.5 0.0 copy-done.2
  75.5 0.0 copy-done
  75.5 1.7 gather_fusion
  77.3 118.5 %all-reduce.4.cloned.1.call-done = bf16[256,8192]{1,0:T(8,128)(2,1)} async-done(((bf16[256,8192]{1,0:T(8,128)(2,1)}), bf16[256,8192]{1,0:T(8,128)(2,1)}) %all-reduce.4.cloned.1.call-update) | async-done | bytes 4194320 | tf_op jit(solution)/shard_map/psum | solution.py:44
  195.8 87.7 %all-gather.7.cloned.1.call-done = bf16[256,8192]{1,0:T(8,128)(2,1)} async-done(((bf16[16,8192]{1,0:T(8,128)(2,1)}), bf16[256,8192]{1,0:T(8,128)(2,1)}) %all-gather.7.cloned.1.call-update) | async-done | bytes 4194320 | tf_op jit(solution)/shard_map/all_gather | solution.py:45
  283.5 4.9 fusion
  288.4 0.0 copy-start.4
  288.5 104.6 %all-gather.9.cloned.1.call-done = bf16[8192,512]{1,0:T(8,128)(2,1)} async-done(((bf16[512,512]{1,0:T(8,128)(2,1)}), bf16[8192,512]{1,0:T(8,128)(2,1)}) %all-gather.9.cloned.1.call-update) | async-done | bytes 8388624 | tf_op jit(solution)/shard_map/all_gather | solution.py:51
  393.1 0.0 copy-done.3
  393.1 8.2 %fusion.20 = f32[256,512]{1,0:T(8,128)S(1)} fusion(bf16[8192,512]{1,0:T(8,128)(2,1)} %all-gather.9.cloned.1.call-done, f32[8192]{0:T(1024)S(1)} %copy-done.3, f32[256]{0:T(256)S(1)} %add_rsqrt_fusion, bf16[256,8192]{1,0:T(8,128)(2,1)} %all-reduce.4.cloned.1.call-done, bf16[256,8192]{1,0:T(8,128)(2,1)} %all-gather.7.cloned.1.call-done), kind=kOutput, calls=%fused_computation.41 | convolution fusion | flops 2164260864 | bytes 17335296 | tf_op jit(solution)/shard_map/dot_general | solution.py:49
  401.3 0.0 copy-done.4
  401.4 0.6 fusion.11
  402.0 38.4 %psum.22 = f32[256]{0:T(256)S(1)} all-reduce(f32[256]{0:T(256)S(1)} %bitcast.53), channel_id=1, replica_groups=mesh['dp'=16,'tensor'=16] {'tensor'}, use_global_device_ids=true, to_apply=%region_2.3 | all-reduce | flops 256 | bytes 2048 | tf_op jit(solution)/shard_map/psum | solution.py:56
  440.3 0.0 copy-start.1
  440.3 23.8 %all-gather.1 = f32[16,1,256]{2,1,0:T(1,128)S(1)} all-gather(f32[1,1,256]{2,1,0:T(1,128)S(1)} %bitcast.51), channel_id=2, replica_groups=mesh['dp'=16,'tensor'=16] {'dp'}, dimensions={0}, use_global_device_ids=true | all-gather | bytes 17408 | tf_op jit(solution)/shard_map/all_gather | solution.py:8
  464.1 1.3 while.14
  465.4 2.1 scatter_custom_fusion
  467.5 0.7 convert_element_type.61
  468.2 0.0 all-reduce.6.cloned.1.call-update
  468.3 0.2 reduce-scatter.2.cloned.1.call-start
  468.5 10.1 %convolution_convert_fusion = bf16[8192,512]{1,0:T(8,128)(2,1)} fusion(f32[256,512]{1,0:T(8,128)S(1)} %fusion.20, f32[512]{0:T(512)S(1)} %copy-done.4, f32[256]{0:T(256)S(1)} %subtract_multiply_fusion, f32[8192]{0:T(1024)S(1)} %copy-done.3, f32[256]{0:T(256)S(1)} %add_rsqrt_fusion, bf16[256,8192]{1,0:T(8,128)(2,1)} %all-reduce.4.cloned.1.call-done, ...), kind=kOutput, calls=%fused_computation.6 | convolution fusion | flops 2169765888 | bytes 17338368 | tf_op jit(solution)/shard_map/dot_general | solution.py:76
  478.6 0.0 copy-done.1
  478.6 0.0 copy-start.5
  478.6 0.0 reduce-scatter.2.cloned.1.call-update
  478.6 0.6 copy-done.5
  479.2 0.6 dynamic-slice
  480.5 0.5 fusion.9
  480.9 49.3 %psum.23 = f32[512]{0:T(512)} all-reduce(f32[512]{0:T(512)S(1)} %bitcast.52), channel_id=1, replica_groups=mesh['dp'=16,'tensor'=16] {'dp'}, use_global_device_ids=true, to_apply=%region_6.7 | all-reduce | flops 512 | bytes 4096 | tf_op jit(solution)/shard_map/psum | solution.py:64
  530.2 113.1 %all-reduce.6.cloned.1.call-done = bf16[128256]{0:T(1024)(128)(2,1)} async-done(((bf16[128256]{0:T(1024)(128)(2,1)}), bf16[128256]{0:T(1024)(128)(2,1)}) %all-reduce.6.cloned.1.call-update) | async-done | bytes 256528
  643.3 1.4 dynamic-slice_convert_fusion
  644.7 144.2 %reduce-scatter.2.cloned.1.call-done = bf16[512,512]{1,0:T(8,128)(2,1)} async-done(((bf16[8192,512]{1,0:T(8,128)(2,1)}), bf16[512,512]{1,0:T(8,128)(2,1)}) %reduce-scatter.2.cloned.1.call-update) | async-done | bytes 524304 | tf_op jit(solution)/shard_map/reduce_scatter | solution.py:75
  788.9 2.1 convert_element_type.60
  (76 shorter events, 0.9 us)
Async XLA Ops:
  7.2 68.4 %copy-start = (f32[128256]{0:T(1024)S(1)}, f32[128256]{0:T(1024)}, u32[]{:S(2)}) copy-start(f32[128256]{0:T(1024)} %param.19) | copy-start | bytes 1539076
  7.2 68.3 %copy-start.2 = (s32[256]{0:T(256)S(1)}, s32[256]{0:T(256)}, u32[]{:S(2)}) copy-start(s32[256]{0:T(256)} %param.12) | copy-start | bytes 3076
  7.2 188.6 %all-reduce.4.cloned.1.call-start = ((), (), s32[]{:S(2)}) async-start(), calls=%async_computation.2 | async-start | bytes 8388608 | tf_op jit(solution)/shard_map/psum | solution.py:44
  15.1 378.0 %copy-start.3 = (f32[8192]{0:T(1024)S(1)}, f32[8192]{0:T(1024)}, u32[]{:S(2)}) copy-start(f32[8192]{0:T(1024)} %param.16) | copy-start | bytes 98308
  15.1 268.4 %all-gather.7.cloned.1.call-start = ((), (), s32[]{:S(2)}) async-start(), calls=%async_computation.1 | async-start | bytes 4456448 | tf_op jit(solution)/shard_map/all_gather | solution.py:45
  15.8 377.3 %all-gather.9.cloned.1.call-start = ((), (), s32[]{:S(2)}) async-start(), calls=%async_computation.3 | async-start | bytes 8912896 | tf_op jit(solution)/shard_map/all_gather | solution.py:51
  16.6 626.7 %all-reduce.6.cloned.1.call-start = ((), (), s32[]{:S(2)}) async-start(), calls=%async_computation.5 | async-start | bytes 516096
  288.4 112.9 %copy-start.4 = (f32[512]{0:T(512)S(1)}, f32[512]{0:T(512)}, u32[]{:S(2)}) copy-start(f32[512]{0:T(512)} %param.18) | copy-start | bytes 6148
  440.3 38.2 %copy-start.1 = (f32[256]{0:T(256)}, f32[256]{0:T(256)S(1)}, u32[]{:S(2)}) copy-start(f32[256]{0:T(256)S(1)} %get-tuple-element.63) | copy-start | bytes 3076
  468.3 320.7 %reduce-scatter.2.cloned.1.call-start = ((), (), s32[]{:S(2)}) async-start(), calls=%async_computation.4 | async-start | bytes 8912896 | tf_op jit(solution)/shard_map/reduce_scatter | solution.py:75
  478.6 0.7 copy-start.5
Sparse Core Ops, SparseCore 0:
  15.2 180.5 all-reduce.3
  197.6 85.8 all-gather.6
  286.2 106.8 all-gather.8
  468.4 174.8 all-reduce.5
  647.8 141.1 reduce-scatter.1
where the time goes:
time: 798 us
  waiting for transfers between devices  570 us (71%)
  blocking collectives  169 us (21%)
  matrix products  27.2 us (3%)
  between operations  15.9 us (2%)
  other arithmetic  11.8 us (1%)
    reduce_scatter x1, waiting for transfers between devices, local(): lax.psum_scatter(lax.dot_general(columns, d_pre, contract, preferred_elem...  144 us
    psum x1, waiting for transfers between devices, local(): lax.psum(partial_sum.astype(jnp.bfloat16), 'tensor').astype(jnp.float32)  119 us
    unnamed x6, waiting for transfers between devices  115 us
    all_gather x1, waiting for transfers between devices, local(): lax.all_gather(twist_in, 'dp', axis=0, tiled=True)  105 us
    all_gather x1, waiting for transfers between devices, local(): resid_all = lax.all_gather(residual, 'tensor', axis=0, tiled=True)  87.7 us
    all_gather x3, blocking collectives, merged_2(): pieces = jax.tree.map(lambda part: lax.all_gather(part, axis), value)  81.4 us
    psum x1, blocking collectives, local(): lax.psum(jnp.dot(weights, active, precision=lax.Precision.HIGHEST), 'dp')  49.3 us
    psum x1, blocking collectives, local(): twist_vals = lax.psum(partial_psi, 'tensor') + token_bias[token_ids]  38.4 us
  transfers between devices with their start and end apart: 5, of which 5 were waited for; matrix products, arithmetic and copies ran while one was open for 2% of the time, Pallas kernels for 0%

commit v1 on v0

--- a/solution.py
+++ b/solution.py
@@ -41,7 +41,8 @@
     seq_len = attn_heads.shape[0]
     vocab_size = token_bias.shape[0]
     partial_sum = jnp.dot(attn_heads, out_proj, preferred_element_type=jnp.float32)
-    summed = lax.psum(partial_sum.astype(jnp.bfloat16), "tensor").astype(jnp.float32)
+    track_slots = lambda frame: lax.all_gather(frame, "tensor").sum(axis=0)
+    summed = track_slots(partial_sum.astype(jnp.bfloat16)).astype(jnp.float32)
     resid_all = lax.all_gather(residual, "tensor", axis=0, tiled=True)
     hidden = (resid_all.astype(jnp.float32) + summed).astype(jnp.bfloat16)
     normed = normalize(hidden, norm_gain)

time: 798 us -> 1310 us (1.64)
  waiting for transfers between devices: 570 us -> 1060 us
  other arithmetic: 11.8 us -> 35.6 us
    all_gather x0 -> x1, waiting for transfers between devices: none -> 629 us  [local(): track_slots = lambda frame: lax.all_gather(frame, 'tensor').sum(axis=0)]
    psum x1 -> x0, waiting for transfers between devices: 119 us -> none  [local(): lax.psum(partial_sum.astype(jnp.bfloat16), 'tensor').astype(jnp.float32)]
    reduce_sum x0 -> x1, other arithmetic: none -> 23.8 us  [local(): track_slots = lambda frame: lax.all_gather(frame, 'tensor').sum(axis=0)]
    all_gather x1, waiting for transfers between devices: 87.7 us -> 65.8 us  [local(): resid_all = lax.all_gather(residual, 'tensor', axis=0, tiled=True)]
  transfers between devices with their start and end apart: 5 -> 5, of which waited for: 5 -> 5; matrix products, arithmetic and copies ran while one was open for 2% -> 3% of each run, Pallas kernels for 0% -> 0%
where the time goes in v1:
time: 1310 us
  waiting for transfers between devices  1060 us (81%)
  blocking collectives  169 us (13%)
  other arithmetic  35.6 us (3%)
  matrix products  27.2 us (2%)
  between operations  15.9 us (1%)
    all_gather x1, waiting for transfers between devices, local(): track_slots = lambda frame: lax.all_gather(frame, 'tensor').sum(axis=0)  629 us
    reduce_scatter x1, waiting for transfers between devices, local(): lax.psum_scatter(lax.dot_general(columns, d_pre, contract, preferred_elem...  144 us
    unnamed x6, waiting for transfers between devices  115 us
    all_gather x1, waiting for transfers between devices, local(): lax.all_gather(twist_in, 'dp', axis=0, tiled=True)  105 us
    all_gather x3, blocking collectives, merged_2(): pieces = jax.tree.map(lambda part: lax.all_gather(part, axis), value)  81.4 us
    all_gather x1, waiting for transfers between devices, local(): resid_all = lax.all_gather(residual, 'tensor', axis=0, tiled=True)  65.8 us
    psum x1, blocking collectives, local(): lax.psum(jnp.dot(weights, active, precision=lax.Precision.HIGHEST), 'dp')  49.3 us
    psum x1, blocking collectives, local(): twist_vals = lax.psum(partial_psi, 'tensor') + token_bias[token_ids]  38.4 us
  transfers between devices with their start and end apart: 5, of which 5 were waited for; matrix products, arithmetic and copies ran while one was open for 3% of the time, Pallas kernels for 0%

profile of v1, /device:TPU:2, one launch (start us, length us, event | category | flops | bytes accessed | tf_op | source)
XLA Modules:
  0.0 1310.0 jit_solution(17498837386184655108)
XLA Ops:
  7.2 0.0 copy-start
  7.2 0.0 copy-start.4
  7.2 0.0 all-gather.13.cloned.1.call-start
  7.2 7.9 convolution_convert_fusion.1
  15.1 0.0 all-gather.13.cloned.1.call-update
  15.1 0.0 all-gather.9.cloned.1.call-start
  15.2 0.7 all-gather.9.cloned.1.call-update
  15.9 0.0 all-gather.11.cloned.1.call-start
  15.9 0.7 all-gather.11.cloned.1.call-update
  16.6 0.0 all-reduce.3.cloned.1.call-start
  18.0 33.4 %all-gather.4 = f32[16,1,256]{2,1,0:T(1,128)S(1)} all-gather(f32[1,1,256]{2,1,0:T(1,128)S(1)} %fusion.13), channel_id=1, replica_groups=mesh['dp'=16,'tensor'=16] {'dp'}, dimensions={0}, use_global_device_ids=true | all-gather | bytes 17408 | tf_op jit(solution)/shard_map/all_gather | solution.py:8
  51.4 0.0 copy-start.1
  51.4 24.1 %all-gather.3 = f32[16,1,256]{2,1,0:T(1,128)S(1)} all-gather(f32[1,1,256]{2,1,0:T(1,128)S(1)} %fusion.14), channel_id=1, replica_groups=mesh['dp'=16,'tensor'=16] {'dp'}, dimensions={0}, use_global_device_ids=true | all-gather | bytes 17408 | tf_op jit(solution)/shard_map/all_gather | solution.py:8
  75.5 0.0 copy-start.2
  75.6 0.0 copy-done.4
  75.6 0.0 copy-done
  75.6 1.7 gather_fusion
  77.3 628.9 %all-gather.13.cloned.1.call-done = bf16[4096,8192]{1,0:T(8,128)(2,1)} async-done(((bf16[256,8192]{1,0:T(8,128)(2,1)}), bf16[4096,8192]{1,0:T(8,128)(2,1)}) %all-gather.13.cloned.1.call-update) | async-done | bytes 67108880 | tf_op jit(solution)/shard_map/all_gather | solution.py:44
  706.2 23.8 %reduce_sum.21 = bf16[256,8192]{1,0:T(8,128)(2,1)} reduce(bf16[16,256,8192]{2,1,0:T(8,128)(2,1)} %bitcast.3, bf16[]{:T(256)} %constant.9.clone.1), dimensions={0}, to_apply=%region_0.0 | reduce | flops 31457280 | bytes 71303168 | tf_op jit(solution)/shard_map/reduce_sum | solution.py:44
  730.1 0.0 copy-done.1
  730.1 0.0 copy-done.2
  730.1 0.0 copy-start.5
  730.1 65.8 %all-gather.9.cloned.1.call-done = bf16[256,8192]{1,0:T(8,128)(2,1)} async-done(((bf16[16,8192]{1,0:T(8,128)(2,1)}), bf16[256,8192]{1,0:T(8,128)(2,1)}) %all-gather.9.cloned.1.call-update) | async-done | bytes 4194320 | tf_op jit(solution)/shard_map/all_gather | solution.py:46
  795.8 4.9 fusion
  800.8 0.0 copy-start.6
  800.8 0.0 slice-start
  800.8 0.0 slice-start.1
  800.8 104.6 %all-gather.11.cloned.1.call-done = bf16[8192,512]{1,0:T(8,128)(2,1)} async-done(((bf16[512,512]{1,0:T(8,128)(2,1)}), bf16[8192,512]{1,0:T(8,128)(2,1)}) %all-gather.11.cloned.1.call-update) | async-done | bytes 8388624 | tf_op jit(solution)/shard_map/all_gather | solution.py:52
  905.4 0.0 copy-done.5
  905.4 8.2 fusion.20
  913.6 0.0 copy-done.6
  913.6 0.6 fusion.11
  914.2 38.4 %psum.14 = f32[256]{0:T(256)S(1)} all-reduce(f32[256]{0:T(256)S(1)} %bitcast.54), channel_id=1, replica_groups=mesh['dp'=16,'tensor'=16] {'tensor'}, use_global_device_ids=true, to_apply=%region_2.3 | all-reduce | flops 256 | bytes 2048 | tf_op jit(solution)/shard_map/psum | solution.py:57
  952.6 0.0 copy-start.3
  952.6 23.8 %all-gather.2 = f32[16,1,256]{2,1,0:T(1,128)S(1)} all-gather(f32[1,1,256]{2,1,0:T(1,128)S(1)} %bitcast.52), channel_id=3, replica_groups=mesh['dp'=16,'tensor'=16] {'dp'}, dimensions={0}, use_global_device_ids=true | all-gather | bytes 17408 | tf_op jit(solution)/shard_map/all_gather | solution.py:8
  976.4 0.0 slice-done
  976.4 0.0 slice-done.1
  976.4 1.3 while.14
  977.7 2.1 scatter_custom_fusion
  979.8 0.7 convert_element_type.63
  980.5 0.0 all-reduce.3.cloned.1.call-update
  980.6 0.2 reduce-scatter.2.cloned.1.call-start
  980.8 10.1 convolution_convert_fusion
  990.9 0.0 copy-done.3
  990.9 0.0 copy-start.7
  990.9 0.0 reduce-scatter.2.cloned.1.call-update
  990.9 0.6 copy-done.7
  991.5 0.6 dynamic-slice
  992.8 0.5 fusion.9
  993.2 49.3 %psum.15 = f32[512]{0:T(512)} all-reduce(f32[512]{0:T(512)S(1)} %bitcast.53), channel_id=1, replica_groups=mesh['dp'=16,'tensor'=16] {'dp'}, use_global_device_ids=true, to_apply=%region_6.7 | all-reduce | flops 512 | bytes 4096 | tf_op jit(solution)/shard_map/psum | solution.py:65
  1042.5 113.2 %all-reduce.3.cloned.1.call-done = bf16[128256]{0:T(1024)(128)(2,1)} async-done(((bf16[128256]{0:T(1024)(128)(2,1)}), bf16[128256]{0:T(1024)(128)(2,1)}) %all-reduce.3.cloned.1.call-update) | async-done | bytes 256528
  1155.7 1.4 dynamic-slice_convert_fusion
  1157.1 144.2 %reduce-scatter.2.cloned.1.call-done = bf16[512,512]{1,0:T(8,128)(2,1)} async-done(((bf16[8192,512]{1,0:T(8,128)(2,1)}), bf16[512,512]{1,0:T(8,128)(2,1)}) %reduce-scatter.2.cloned.1.call-update) | async-done | bytes 524304 | tf_op jit(solution)/shard_map/reduce_scatter | solution.py:76
  1301.3 2.1 convert_element_type.62
  (74 shorter events, 0.9 us)
Async XLA Ops:
  7.2 68.4 %copy-start = (f32[128256]{0:T(1024)S(1)}, f32[128256]{0:T(1024)}, u32[]{:S(2)}) copy-start(f32[128256]{0:T(1024)} %param.19) | copy-start | bytes 1539076
  7.2 68.4 %copy-start.4 = (s32[256]{0:T(256)S(1)}, s32[256]{0:T(256)}, u32[]{:S(2)}) copy-start(s32[256]{0:T(256)} %param.12) | copy-start | bytes 3076
  7.2 699.0 %all-gather.13.cloned.1.call-start = ((), (), s32[]{:S(2)}) async-start(), calls=%async_computation.4 | async-start | bytes 71303168 | tf_op jit(solution)/shard_map/all_gather | solution.py:44
  15.1 780.7 %all-gather.9.cloned.1.call-start = ((), (), s32[]{:S(2)}) async-start(), calls=%async_computation.1 | async-start | bytes 4456448 | tf_op jit(solution)/shard_map/all_gather | solution.py:46
  15.9 889.5 %all-gather.11.cloned.1.call-start = ((), (), s32[]{:S(2)}) async-start(), calls=%async_computation.2 | async-start | bytes 8912896 | tf_op jit(solution)/shard_map/all_gather | solution.py:52
  16.6 1139.1 %all-reduce.3.cloned.1.call-start = ((), (), s32[]{:S(2)}) async-start(), calls=%async_computation.5 | async-start | bytes 516096
  51.4 678.7 %copy-start.1 = (f32[16,1,256]{2,1,0:T(1,128)}, f32[16,1,256]{2,1,0:T(1,128)S(1)}, u32[]{:S(2)}) copy-start(f32[16,1,256]{2,1,0:T(1,128)S(1)} %all-gather.4) | copy-start | bytes 49156
  75.5 654.5 %copy-start.2 = (f32[16,1,256]{2,1,0:T(1,128)}, f32[16,1,256]{2,1,0:T(1,128)S(1)}, u32[]{:S(2)}) copy-start(f32[16,1,256]{2,1,0:T(1,128)S(1)} %all-gather.3) | copy-start | bytes 49156
  730.1 175.3 %copy-start.5 = (f32[8192]{0:T(1024)S(1)}, f32[8192]{0:T(1024)}, u32[]{:S(2)}) copy-start(f32[8192]{0:T(1024)} %param.16) | copy-start | bytes 98308
  800.8 112.9 %copy-start.6 = (f32[512]{0:T(512)S(1)}, f32[512]{0:T(512)}, u32[]{:S(2)}) copy-start(f32[512]{0:T(512)} %param.18) | copy-start | bytes 6148
  800.8 175.7 %slice-start = ((f32[16,1,256]{2,1,0:T(1,128)}), f32[1,1,256]{2,1,0:T(1,128)S(1)}, s32[]{:S(2)}) async-start(f32[16,1,256]{2,1,0:T(1,128)} %copy-done.1), calls=%async_computation.6 | async-start | bytes 2048 | tf_op jit(solution)/shard_map/slice | solution.py:9
  800.8 175.6 %slice-start.1 = ((f32[16,1,256]{2,1,0:T(1,128)}), f32[1,1,256]{2,1,0:T(1,128)S(1)}, s32[]{:S(2)}) async-start(f32[16,1,256]{2,1,0:T(1,128)} %copy-done.2), calls=%async_computation.7 | async-start | bytes 2048 | tf_op jit(solution)/shard_map/slice | solution.py:9
  952.6 38.3 %copy-start.3 = (f32[256]{0:T(256)}, f32[256]{0:T(256)S(1)}, u32[]{:S(2)}) copy-start(f32[256]{0:T(256)S(1)} %get-tuple-element.63) | copy-start | bytes 3076
  980.6 320.8 %reduce-scatter.2.cloned.1.call-start = ((), (), s32[]{:S(2)}) async-start(), calls=%async_computation.3 | async-start | bytes 8912896 | tf_op jit(solution)/shard_map/reduce_scatter | solution.py:76
  990.9 0.7 copy-start.7
Sparse Core Ops, SparseCore 0:
  15.3 690.9 all-gather.12
  708.0 87.7 all-gather.8
  798.5 106.8 all-gather.10
  980.7 174.9 all-reduce.2
  1160.2 141.1 reduce-scatter.1
